TPU v7x, 32 devices: a whole 2x2x4 slice. The times are simulated.
32 devices in a mesh: group: 2 (over x), dev: 16 (over z, y, core).
Axes of the slice: x: 2, y: 2, z: 4, core: 2. Of those that a mesh axis runs over, the one named last changes fastest.
Arguments:
- suffix_x: bfloat16 [2, 4096, 1600], P('group', 'dev'), may hold values from -6 to 6
- suffix_query: bfloat16 [2, 4096, 1024], P('group', 'dev'), may hold values from -128 to 128
- suffix_keyval: bfloat16 [2, 4096, 2048], P('group', 'dev'), may hold values from -6 to 6
- prefix_keyval: bfloat16 [2, 128, 2048], P('group', 'dev'), may hold values from -6 to 6
- prefix_hidden: bfloat16 [2, 128, 1600], P('group', 'dev'), may hold values from -6 to 6
- kv_weight: bfloat16 [1600, 2048], replicated, may hold values from -0.15625 to 0.15625
- out_weight: bfloat16 [1024, 1600], replicated, may hold values from -0.1875 to 0.1875
- fc_weight: bfloat16 [1600, 3840], P(None, ('group', 'dev')), may hold values from -0.15625 to 0.15625
- proj_weight: bfloat16 [3840, 1600], P(('group', 'dev')), may hold values from -0.09375 to 0.09375
- lengths: int32 [2, 16], P('group'), may hold values from 1 to 256, 2048 in all within a row
- placement: int32 [2, 16], P('group'), may hold values from 0 to 15, each once within a row
- owners: int32 [2, 16], P('group'), may hold values from 0 to 15, each once within a row
- recompute: int32 [2, 2], P('group'), may hold values from 0 to 15
Outputs:
- layer_out: bfloat16 [2, 4096, 1600], P('group', 'dev')
All inputs are finite; a program needn't handle non-finite values.
Results may differ from a plain program's by a relative error of at most 0.008.
Values may be sent and summed in bfloat16 or wider, within the bound.
No kernel may reach another device: no remote copies, remote signals or barrier semaphores. Data moves between devices by JAX's collectives and lax.ppermute only.
A program may use at most 128 MiB of HBM per device.

v0:
```python
import jax
import jax.numpy as jnp
from jax import lax
from jax.sharding import PartitionSpec as P

HEAD_DIM = 64
NEGATIVE = -1e30
EPSILON = 1e-05
SCORE_SCALE = 0.125


def normalize(values_in):
    values_in = values_in.astype(jnp.float32)
    average = jnp.mean(values_in, axis=-1, keepdims=True)
    centered = values_in - average
    variance = jnp.mean(centered * centered, axis=-1, keepdims=True)
    return centered / jnp.sqrt(variance + EPSILON)


def absorb(state, queries, keyval, allowed):
    running_top, running_total, accumulated = state
    head_count = queries.shape[1]
    head_size = queries.shape[2]
    row_count = keyval.shape[0]
    width_att = head_count * head_size
    key_rows = keyval[:, :width_att].reshape(row_count, head_count, head_size)
    val_rows = keyval[:, width_att:].reshape(row_count, head_count, head_size)
    scores = (
        jnp.einsum("qhd,khd->hqk", queries, key_rows, preferred_element_type=jnp.float32)
        * SCORE_SCALE
    )
    scores = jnp.where(allowed[None], scores, NEGATIVE)
    new_top = jnp.maximum(running_top, jnp.max(scores, axis=-1))
    factor = jnp.exp(running_top - new_top)
    weights = jnp.where(allowed[None], jnp.exp(scores - new_top[:, :, None]), 0.0)
    running_total = running_total * factor + jnp.sum(weights, axis=-1)
    weights_low = weights.astype(jnp.bfloat16)
    update = jnp.einsum("hqk,khd->qhd", weights_low, val_rows, preferred_element_type=jnp.float32)
    accumulated = accumulated * jnp.transpose(factor)[:, :, None] + update
    return (new_top, running_total, accumulated)


def per_device(
    suffix_x,
    suffix_query,
    suffix_keyval,
    prefix_keyval,
    prefix_hidden,
    kv_weight,
    out_weight,
    fc_weight,
    proj_weight,
    lengths,
    placement,
    owners,
    recompute,
):
    device_count = lax.axis_size("dev")
    my_device = lax.axis_index("dev")
    slots = suffix_x.shape[1]
    block_rows = prefix_keyval.shape[1]
    width_att = suffix_query.shape[2]
    head_count = width_att // HEAD_DIM
    device_ids = jnp.arange(device_count, dtype=jnp.int32)
    hits = placement[0][:, None] == device_ids[None, :]
    device_length = jnp.sum(jnp.where(hits, lengths[0][:, None], 0), axis=0)
    my_length = jnp.sum(jnp.where(device_ids == my_device, device_length, 0))
    block_ids = jnp.arange(owners.shape[1], dtype=jnp.int32)
    chosen = recompute[0]
    chosen_owner = jnp.sum(
        jnp.where(chosen[:, None] == block_ids[None, :], owners[0][None, :], 0), axis=1
    )
    stale_device = jnp.any(chosen_owner[:, None] == device_ids[None, :], axis=0)
    queries = suffix_query[0].reshape(slots, head_count, HEAD_DIM)
    normed_prefix = normalize(prefix_hidden[0]).astype(jnp.bfloat16)
    fresh = jnp.dot(normed_prefix, kv_weight, preferred_element_type=jnp.float32).astype(
        jnp.bfloat16
    )
    my_stale = jnp.any(chosen_owner == my_device)
    local_kv = jnp.where(my_stale, fresh, prefix_keyval[0])
    skip_device = jnp.zeros_like(stale_device)
    gathered = lax.all_gather(local_kv, "dev", axis=0, tiled=True)
    prefix_count = gathered.shape[0]
    row_device = jnp.arange(prefix_count, dtype=jnp.int32) // block_rows
    skipped = jnp.any((row_device[:, None] == device_ids[None, :]) & skip_device[None, :], axis=1)
    state = (
        jnp.full((head_count, slots), NEGATIVE, jnp.float32),
        jnp.zeros((head_count, slots), jnp.float32),
        jnp.zeros((slots, head_count, HEAD_DIM), jnp.float32),
    )
    key_block = 512 if prefix_count % 512 == 0 else prefix_count
    for block_start in range(0, prefix_count, key_block):
        kept = jnp.logical_not(skipped[block_start : block_start + key_block])
        allowed = jnp.broadcast_to(kept[None, :], (slots, key_block))
        state = absorb(state, queries, gathered[block_start : block_start + key_block], allowed)
    positions = jnp.arange(slots, dtype=jnp.int32)
    causal = (positions[None, :] <= positions[:, None]) & (positions[None, :] < my_length)
    state = absorb(state, queries, suffix_keyval[0], causal)
    final_top, final_total, accumulated = state
    attended = (
        (accumulated / jnp.transpose(final_total)[:, :, None])
        .reshape(slots, width_att)
        .astype(jnp.bfloat16)
    )
    projected = jnp.dot(attended, out_weight, preferred_element_type=jnp.float32)
    residual = suffix_x[0].astype(jnp.float32) + projected
    normed = normalize(residual).astype(jnp.bfloat16)
    fc_full, proj_full = (
        lax.all_gather(fc_weight, ("group", "dev"), axis=1, tiled=True),
        lax.all_gather(proj_weight, ("group", "dev"), axis=0, tiled=True),
    )
    inner = jnp.dot(normed, fc_full, preferred_element_type=jnp.float32)
    activated = jax.nn.gelu(inner, approximate=True).astype(jnp.bfloat16)
    feed_out = jnp.dot(activated, proj_full, preferred_element_type=jnp.float32)
    live = positions[:, None] < my_length
    return jnp.where(live, residual + feed_out, 0.0).astype(jnp.bfloat16)[None]


def solution(mesh):
    return jax.shard_map(
        per_device,
        mesh=mesh,
        in_specs=(
            P("group", "dev", None),
            P("group", "dev", None),
            P("group", "dev", None),
            P("group", "dev", None),
            P("group", "dev", None),
            P(),
            P(),
            P(None, ("group", "dev")),
            P(("group", "dev"), None),
            P("group", None),
            P("group", None),
            P("group", None),
            P("group", None),
        ),
        out_specs=P("group", "dev", None),
        check_vma=False,
    )
```

profile of v0, /device:TPU:0, one launch (start us, length us, event | category | flops | bytes accessed | tf_op | source)
XLA Modules:
  0.0 235.2 jit_solution(8602153443183435182)
XLA Ops:
  6.6 0.7 all-gather.3.cloned.1.call-update
  7.3 0.7 all-gather.5.cloned.1.call-update
  8.0 2.2 fusion.67
  10.3 2.0 copy.33
  12.3 2.1 copy.30
  14.6 0.6 compare_reduce_fusion
  15.6 4.5 %fusion.14 = bf16[8,2048]{1,0:T(8,128)(2,1)S(1)} fusion(bf16[1600,2048]{1,0:T(8,128)(2,1)} %param.18, bf16[1,8,2048]{2,1,0:T(8,128)(2,1)S(1)} %copy-done.5, pred[]{:T(512)} %compare_reduce_fusion, bf16[1,8,1600]{2,1,0:T(8,128)(2,1)S(1)} %copy-done.4, f32[8]{0:T(128)S(1)} %add_sqrt_fusion.1, f32[8]{0:T(128)S(1)} %broadcast_multiply_fusion.1), kind=kOutput, calls=%fused_computation.20 | convolution fusion | flops 52512768 | bytes 6644801 | tf_op jit(solution)/shard_map/dot_general | solution.py:76
  20.1 25.2 %all_gather.9 = bf16[128,2048]{1,0:T(8,128)(2,1)S(1)} all-gather(bf16[8,2048]{1,0:T(8,128)(2,1)S(1)} %fusion.14), channel_id=1, replica_groups=mesh['group'=2,'dev'=16] {'dev'}, dimensions={0}, use_global_device_ids=true | all-gather | bytes 557056 | tf_op jit(solution)/shard_map/all_gather | solution.py:82
  45.3 0.7 fusion.68
  46.1 1.8 copy.29
  47.9 2.0 copy.34
  49.9 0.8 copy.31
  50.8 0.6 fusion.56
  51.5 0.6 iota_compare_fusion.2
  52.2 1.6 bitcast_reduce_fusion
  53.9 2.0 fusion.8
  56.3 1.0 fusion.9
  57.3 1.1 fusion.26
  58.5 0.6 fusion.33
  59.6 1.1 fusion.69
  60.7 1.2 copy-done.1
  62.2 49.0 %all-gather.3.cloned.1.call-done = bf16[1600,3840]{0,1:T(8,128)(2,1)} async-done(((bf16[1600,120]{0,1:T(8,128)(2,1)}), bf16[1600,3840]{0,1:T(8,128)(2,1)}) %all-gather.3.cloned.1.call-update) | async-done | bytes 12288016 | tf_op jit(solution)/shard_map/all_gather | solution.py:109
  111.2 98.2 %all-gather.5.cloned.1.call-done = bf16[3840,1600]{1,0:T(8,128)(2,1)} async-done(((bf16[120,1600]{1,0:T(8,128)(2,1)}), bf16[3840,1600]{1,0:T(8,128)(2,1)}) %all-gather.5.cloned.1.call-update) | async-done | bytes 12288016 | tf_op jit(solution)/shard_map/all_gather | solution.py:110
  209.4 19.0 %fusion.13 = bf16[1,256,1600]{1,2,0:T(8,128)(2,1)} fusion(f32[256,1600]{0,1:T(8,128)} %copy-done.1, bf16[3840,1600]{1,0:T(8,128)(2,1)} %all-gather.5.cloned.1.call-done, bf16[1600,3840]{0,1:T(8,128)(2,1)} %all-gather.3.cloned.1.call-done, f32[256]{0:T(256)S(1)} %add_sqrt_fusion, f32[256]{0:T(256)S(1)} %broadcast_multiply_fusion, ...), kind=kOutput, calls=%fused_computation.18 | convolution fusion | flops 6302760960 | bytes 27035904 | tf_op jit(solution)/shard_map/dot_general | solution.py:114
  (36 shorter events, 2.0 us)
Async XLA Ops:
  6.5 52.6 %copy-start = (bf16[1024,1600]{0,1:T(8,128)(2,1)S(1)}, bf16[1024,1600]{0,1:T(8,128)(2,1)}, u32[]{:S(2)}) copy-start(bf16[1024,1600]{0,1:T(8,128)(2,1)} %param.19) | copy-start | bytes 9830404
  6.5 7.9 %copy-start.8 = (s32[1,2]{1,0:T(1,128)S(1)}, s32[1,2]{1,0:T(1,128)}, u32[]{:S(2)}) copy-start(s32[1,2]{1,0:T(1,128)} %param.25) | copy-start | bytes 28
  6.5 7.9 %copy-start.7 = (s32[1,16]{1,0:T(1,128)S(1)}, s32[1,16]{1,0:T(1,128)}, u32[]{:S(2)}) copy-start(s32[1,16]{1,0:T(1,128)} %param.24) | copy-start | bytes 196
  6.5 8.7 %copy-start.4 = (bf16[1,8,1600]{2,1,0:T(8,128)(2,1)S(1)}, bf16[1,8,1600]{2,1,0:T(8,128)(2,1)}, u32[]{:S(2)}) copy-start(bf16[1,8,1600]{2,1,0:T(8,128)(2,1)} %param.17) | copy-start | bytes 76804
  6.5 9.1 %copy-start.5 = (bf16[1,8,2048]{2,1,0:T(8,128)(2,1)S(1)}, bf16[1,8,2048]{2,1,0:T(8,128)(2,1)}, u32[]{:S(2)}) copy-start(bf16[1,8,2048]{2,1,0:T(8,128)(2,1)} %param.16) | copy-start | bytes 98308
  6.5 104.7 %all-gather.3.cloned.1.call-start = ((), (), s32[]{:S(2)}) async-start(), calls=%async_computation | async-start | bytes 13178880 | tf_op jit(solution)/shard_map/all_gather | solution.py:109
  7.3 202.1 %all-gather.5.cloned.1.call-start = ((), (), s32[]{:S(2)}) async-start(), calls=%async_computation.1 | async-start | bytes 13178880 | tf_op jit(solution)/shard_map/all_gather | solution.py:110
  15.6 35.2 %copy-start.9 = (s32[1,16]{1,0:T(1,128)S(1)}, s32[1,16]{1,0:T(1,128)}, u32[]{:S(2)}) copy-start(s32[1,16]{1,0:T(1,128)} %param.22) | copy-start | bytes 196
  15.6 35.1 %copy-start.10 = (s32[1,16]{1,0:T(1,128)S(1)}, s32[1,16]{1,0:T(1,128)}, u32[]{:S(2)}) copy-start(s32[1,16]{1,0:T(1,128)} %param.23) | copy-start | bytes 196
  55.9 1.4 copy-start.2
  57.3 1.1 copy-start.3
  58.5 1.2 copy-start.6
  60.7 1.2 copy-start.1
Sparse Core Ops, SparseCore 0:
  10.2 100.9 all-gather.2
  114.0 95.2 all-gather.4
where the time goes:
time: 236 us; the launch traced here: 235 us
  waiting for transfers between devices  149 us (63%)
  matrix products  29.9 us (13%)
  blocking collectives  25.2 us (11%)
  local copies, waits for them, and re-layouts  13.6 us (6%)
  between operations  13.6 us (6%)
  other arithmetic  4.28 us (2%)
    all_gather x1, waiting for transfers between devices, per_device(): lax.all_gather(proj_weight, ('group', 'dev'), axis=0, tiled=True)  98.2 us
    all_gather x1, waiting for transfers between devices, per_device(): lax.all_gather(fc_weight, ('group', 'dev'), axis=1, tiled=True)  49 us
    all_gather x1, blocking collectives, per_device(): gathered = lax.all_gather(local_kv, 'dev', axis=0, tiled=True)  25.2 us
    dot_general x1, matrix products, per_device(): feed_out = jnp.dot(activated, proj_full, preferred_element_type=jnp.float32)  19 us
    slice x3, local copies, waits for them, and re-layouts, absorb(): key_rows = keyval[:, :width_att].reshape(row_count, head_count, head_size)  6.07 us
  transfers between devices with their start and end apart: 2, of which 2 were waited for; matrix products, arithmetic and copies ran while one was open for 11% of the time, Pallas kernels for 0%

commit v1 on v0

--- a/solution.py
+++ b/solution.py
@@ -79,7 +79,12 @@
     my_stale = jnp.any(chosen_owner == my_device)
     local_kv = jnp.where(my_stale, fresh, prefix_keyval[0])
     skip_device = jnp.zeros_like(stale_device)
-    gathered = lax.all_gather(local_kv, "dev", axis=0, tiled=True)
+    ring = [local_kv]
+    for hop in range(15):
+        ring.append(lax.ppermute(ring[-1], "dev", [(dev, (dev + 1) % 16) for dev in range(16)]))
+    gathered = jnp.roll(
+        jnp.concatenate(ring[::-1], axis=0), (lax.axis_index("dev") + 1) * ring[0].shape[0], axis=0
+    )
     prefix_count = gathered.shape[0]
     row_device = jnp.arange(prefix_count, dtype=jnp.int32) // block_rows
     skipped = jnp.any((row_device[:, None] == device_ids[None, :]) & skip_device[None, :], axis=1)

time: 236 us -> 239 us (1.013)
  blocking collectives: 25.2 us -> 0 us
  local copies, waits for them, and re-layouts: 13.6 us -> 29.7 us
  waiting for transfers between devices: 149 us -> 154 us
    ppermute x0 -> x15, waiting for transfers between devices: none -> 86 us  [per_device(): lax.ppermute(ring[-1], 'dev', [(dev, (dev + 1) % 16) for dev in range(16)])]
    all_gather x1, waiting for transfers between devices: 49 us -> 0.01 us  [per_device(): lax.all_gather(fc_weight, ('group', 'dev'), axis=1, tiled=True)]
    all_gather x1, waiting for transfers between devices: 98.2 us -> 66.5 us  [per_device(): lax.all_gather(proj_weight, ('group', 'dev'), axis=0, tiled=True)]
    all_gather x1 -> x0, blocking collectives: 25.2 us -> none  [per_device(): gathered = lax.all_gather(local_kv, 'dev', axis=0, tiled=True)]
    unnamed x23 -> x72, local copies, waits for them, and re-layouts: 3.87 us -> 21.2 us
  transfers between devices with their start and end apart: 2 -> 17, of which waited for: 2 -> 16; matrix products, arithmetic and copies ran while one was open for 11% -> 19% of each run, Pallas kernels for 0% -> 0%
where the time goes in v1:
time: 239 us; the launch traced here: 237 us
  waiting for transfers between devices  154 us (64%)
  matrix products  32.2 us (13%)
  local copies, waits for them, and re-layouts  29.7 us (12%)
  between operations  13.7 us (6%)
  other arithmetic  6.55 us (3%)
    ppermute x15, waiting for transfers between devices, per_device(): lax.ppermute(ring[-1], 'dev', [(dev, (dev + 1) % 16) for dev in range(16)])  86 us
    all_gather x1, waiting for transfers between devices, per_device(): lax.all_gather(proj_weight, ('group', 'dev'), axis=0, tiled=True)  66.5 us
    unnamed x72, local copies, waits for them, and re-layouts  21.2 us
    dot_general x1, matrix products, per_device(): feed_out = jnp.dot(activated, proj_full, preferred_element_type=jnp.float32)  19.1 us
    dot_general x2, matrix products, absorb(): jnp.einsum('qhd,khd->hqk', queries, key_rows, preferred_element_type=jnp....  5.79 us
    slice x3, local copies, waits for them, and re-layouts, absorb(): key_rows = keyval[:, :width_att].reshape(row_count, head_count, head_size)  4.9 us
  transfers between devices with their start and end apart: 17, of which 16 were waited for; matrix products, arithmetic and copies ran while one was open for 19% of the time, Pallas kernels for 0%

profile of v1, /device:TPU:0, one launch (start us, length us, event | category | flops | bytes accessed | tf_op | source)
XLA Modules:
  0.0 236.7 jit_solution(15565037317143698968)
XLA Ops:
  11.4 4.5 %fusion.14 = bf16[8,2048]{1,0:T(8,128)(2,1)S(1)} fusion(bf16[1600,2048]{1,0:T(8,128)(2,1)} %param.18, bf16[1,8,2048]{2,1,0:T(8,128)(2,1)} %param.16, pred[]{:T(512)} %compare_reduce_fusion, bf16[1,8,1600]{2,1,0:T(8,128)(2,1)} %param.17, f32[8]{0:T(128)S(1)} %add_sqrt_fusion.1, f32[8]{0:T(128)S(1)} %broadcast_multiply_fusion.1), kind=kOutput, calls=%fused_computation.20 | convolution fusion | flops 52512768 | bytes 6644801 | tf_op jit(solution)/shard_map/dot_general | solution.py:76
  16.4 6.6 %collective-permute-done = bf16[8,2048]{1,0:T(8,128)(2,1)S(1)} collective-permute-done((bf16[8,2048]{1,0:T(8,128)(2,1)S(1)}, bf16[8,2048]{1,0:T(8,128)(2,1)S(1)}, u32[]{:S(2)}, u32[]{:S(2)}) %collective-permute-start) | collective-permute-done | bytes 32800 | tf_op jit(solution)/shard_map/ppermute | solution.py:84
  23.0 6.5 %collective-permute-done.1 = bf16[8,2048]{1,0:T(8,128)(2,1)S(1)} collective-permute-done((bf16[8,2048]{1,0:T(8,128)(2,1)S(1)}, bf16[8,2048]{1,0:T(8,128)(2,1)S(1)}, u32[]{:S(2)}, u32[]{:S(2)}) %collective-permute-start.1) | collective-permute-done | bytes 32800 | tf_op jit(solution)/shard_map/ppermute | solution.py:84
  29.6 6.6 %collective-permute-done.2 = bf16[8,2048]{1,0:T(8,128)(2,1)S(1)} collective-permute-done((bf16[8,2048]{1,0:T(8,128)(2,1)S(1)}, bf16[8,2048]{1,0:T(8,128)(2,1)S(1)}, u32[]{:S(2)}, u32[]{:S(2)}) %collective-permute-start.2) | collective-permute-done | bytes 32800 | tf_op jit(solution)/shard_map/ppermute | solution.py:84
  36.1 6.0 %collective-permute-done.3 = bf16[8,2048]{1,0:T(8,128)(2,1)S(1)} collective-permute-done((bf16[8,2048]{1,0:T(8,128)(2,1)S(1)}, bf16[8,2048]{1,0:T(8,128)(2,1)S(1)}, u32[]{:S(2)}, u32[]{:S(2)}) %collective-permute-start.3) | collective-permute-done | bytes 32800 | tf_op jit(solution)/shard_map/ppermute | solution.py:84
  42.2 6.8 %collective-permute-done.4 = bf16[8,2048]{1,0:T(8,128)(2,1)S(1)} collective-permute-done((bf16[8,2048]{1,0:T(8,128)(2,1)S(1)}, bf16[8,2048]{1,0:T(8,128)(2,1)S(1)}, u32[]{:S(2)}, u32[]{:S(2)}) %collective-permute-start.4) | collective-permute-done | bytes 32800 | tf_op jit(solution)/shard_map/ppermute | solution.py:84
  48.9 6.7 %collective-permute-done.5 = bf16[8,2048]{1,0:T(8,128)(2,1)S(1)} collective-permute-done((bf16[8,2048]{1,0:T(8,128)(2,1)S(1)}, bf16[8,2048]{1,0:T(8,128)(2,1)S(1)}, u32[]{:S(2)}, u32[]{:S(2)}) %collective-permute-start.5) | collective-permute-done | bytes 32800 | tf_op jit(solution)/shard_map/ppermute | solution.py:84
  56.2 6.6 %collective-permute-done.6 = bf16[8,2048]{1,0:T(8,128)(2,1)S(1)} collective-permute-done((bf16[8,2048]{1,0:T(8,128)(2,1)S(1)}, bf16[8,2048]{1,0:T(8,128)(2,1)S(1)}, u32[]{:S(2)}, u32[]{:S(2)}) %collective-permute-start.6) | collective-permute-done | bytes 32800 | tf_op jit(solution)/shard_map/ppermute | solution.py:84
  63.4 6.0 %collective-permute-done.7 = bf16[8,2048]{1,0:T(8,128)(2,1)S(1)} collective-permute-done((bf16[8,2048]{1,0:T(8,128)(2,1)S(1)}, bf16[8,2048]{1,0:T(8,128)(2,1)S(1)}, u32[]{:S(2)}, u32[]{:S(2)}) %collective-permute-start.7) | collective-permute-done | bytes 32800 | tf_op jit(solution)/shard_map/ppermute | solution.py:84
  70.1 6.7 %collective-permute-done.8 = bf16[8,2048]{1,0:T(8,128)(2,1)S(1)} collective-permute-done((bf16[8,2048]{1,0:T(8,128)(2,1)S(1)}, bf16[8,2048]{1,0:T(8,128)(2,1)S(1)}, u32[]{:S(2)}, u32[]{:S(2)}) %collective-permute-start.8) | collective-permute-done | bytes 32800 | tf_op jit(solution)/shard_map/ppermute | solution.py:84
  77.9 5.6 %collective-permute-done.9 = bf16[8,2048]{1,0:T(8,128)(2,1)S(1)} collective-permute-done((bf16[8,2048]{1,0:T(8,128)(2,1)S(1)}, bf16[8,2048]{1,0:T(8,128)(2,1)S(1)}, u32[]{:S(2)}, u32[]{:S(2)}) %collective-permute-start.9) | collective-permute-done | bytes 32800 | tf_op jit(solution)/shard_map/ppermute | solution.py:84
  83.6 6.6 %collective-permute-done.10 = bf16[8,2048]{1,0:T(8,128)(2,1)S(1)} collective-permute-done((bf16[8,2048]{1,0:T(8,128)(2,1)S(1)}, bf16[8,2048]{1,0:T(8,128)(2,1)S(1)}, u32[]{:S(2)}, u32[]{:S(2)}) %collective-permute-start.10) | collective-permute-done | bytes 32800 | tf_op jit(solution)/shard_map/ppermute | solution.py:84
  90.9 6.0 %collective-permute-done.11 = bf16[8,2048]{1,0:T(8,128)(2,1)S(1)} collective-permute-done((bf16[8,2048]{1,0:T(8,128)(2,1)S(1)}, bf16[8,2048]{1,0:T(8,128)(2,1)S(1)}, u32[]{:S(2)}, u32[]{:S(2)}) %collective-permute-start.11) | collective-permute-done | bytes 32800 | tf_op jit(solution)/shard_map/ppermute | solution.py:84
  97.6 6.2 %collective-permute-done.12 = bf16[8,2048]{1,0:T(8,128)(2,1)} collective-permute-done((bf16[8,2048]{1,0:T(8,128)(2,1)S(1)}, bf16[8,2048]{1,0:T(8,128)(2,1)}, u32[]{:S(2)}, u32[]{:S(2)}) %collective-permute-start.12) | collective-permute-done | bytes 32800 | tf_op jit(solution)/shard_map/ppermute | solution.py:84
  104.0 2.1 copy.30
  106.1 2.0 copy.33
  108.1 2.7 %collective-permute-done.13 = bf16[8,2048]{1,0:T(8,128)(2,1)} collective-permute-done((bf16[8,2048]{1,0:T(8,128)(2,1)}, bf16[8,2048]{1,0:T(8,128)(2,1)}, u32[]{:S(2)}, u32[]{:S(2)}) %collective-permute-start.13) | collective-permute-done | bytes 32800 | tf_op jit(solution)/shard_map/ppermute | solution.py:84
  110.8 4.0 %fusion.8 = (f32[16,256]{1,0:T(8,128)S(1)}, f32[16,256,256]{1,2,0:T(8,128)}) fusion(pred[256,256]{0,1:T(8,128)(4,1)S(1)} %fusion.42, bf16[256,16,64]{0,2,1:T(8,128)(2,1)} %bitcast.87, bf16[256,16,64]{0,2,1:T(8,128)(2,1)} %bitcast.89), kind=kOutput, calls=%fused_computation.11 | convolution fusion | flops 137359360 | bytes 5324800 | tf_op jit(solution)/shard_map/qhd,khd->hqk/dot_general | solution.py:29
  114.9 2.0 copy.34
  133.3 1.8 copy.29
  135.9 1.8 bitcast_reduce_fusion
  142.7 1.2 copy-done.2
  144.2 66.5 %all-gather.5.cloned.1.call-done = bf16[3840,1600]{1,0:T(8,128)(2,1)} async-done(((bf16[120,1600]{1,0:T(8,128)(2,1)}), bf16[3840,1600]{1,0:T(8,128)(2,1)}) %all-gather.5.cloned.1.call-update) | async-done | bytes 12288016 | tf_op jit(solution)/shard_map/all_gather | solution.py:115
  210.7 19.1 %fusion.13 = bf16[1,256,1600]{1,2,0:T(8,128)(2,1)} fusion(f32[256,1600]{0,1:T(8,128)} %copy-done.2, bf16[3840,1600]{1,0:T(8,128)(2,1)} %all-gather.5.cloned.1.call-done, bf16[1600,3840]{0,1:T(8,128)(2,1)} %all-gather.3.cloned.1.call-done, f32[256]{0:T(256)S(1)} %add_sqrt_fusion, f32[256]{0:T(256)S(1)} %broadcast_multiply_fusion, ...), kind=kOutput, calls=%fused_computation.18 | convolution fusion | flops 6302760960 | bytes 27035904 | tf_op jit(solution)/shard_map/dot_general | solution.py:119
  (115 shorter events, 32.1 us)
Async XLA Ops:
  6.5 134.6 %copy-start = (bf16[1024,1600]{0,1:T(8,128)(2,1)S(1)}, bf16[1024,1600]{0,1:T(8,128)(2,1)}, u32[]{:S(2)}) copy-start(bf16[1024,1600]{0,1:T(8,128)(2,1)} %param.19) | copy-start | bytes 9830404
  6.5 137.7 %all-gather.3.cloned.1.call-start = ((), (), s32[]{:S(2)}) async-start(), calls=%async_computation | async-start | bytes 13178880 | tf_op jit(solution)/shard_map/all_gather | solution.py:114
  7.3 203.5 %all-gather.5.cloned.1.call-start = ((), (), s32[]{:S(2)}) async-start(), calls=%async_computation.1 | async-start | bytes 13178880 | tf_op jit(solution)/shard_map/all_gather | solution.py:115
  8.0 68.8 %copy-start.3 = (bf16[1,256,2048]{2,1,0:T(8,128)(2,1)S(1)}, bf16[1,256,2048]{2,1,0:T(8,128)(2,1)}, u32[]{:S(2)}) copy-start(bf16[1,256,2048]{2,1,0:T(8,128)(2,1)} %param.15) | copy-start | bytes 3145732
  11.4 72.1 %copy-start.18 = (s32[1,16]{1,0:T(1,128)S(1)}, s32[1,16]{1,0:T(1,128)}, u32[]{:S(2)}) copy-start(s32[1,16]{1,0:T(1,128)} %param.22) | copy-start | bytes 196
  11.4 72.1 %copy-start.19 = (s32[1,16]{1,0:T(1,128)S(1)}, s32[1,16]{1,0:T(1,128)}, u32[]{:S(2)}) copy-start(s32[1,16]{1,0:T(1,128)} %param.23) | copy-start | bytes 196
  16.0 7.0 %collective-permute-start = (bf16[8,2048]{1,0:T(8,128)(2,1)S(1)}, bf16[8,2048]{1,0:T(8,128)(2,1)S(1)}, u32[]{:S(2)}, u32[]{:S(2)}) collective-permute-start(bf16[8,2048]{1,0:T(8,128)(2,1)S(1)} %fusion.14), channel_id=1, source_target_pairs={{0,1},{1,2},{2,3},{3,4},{4,5},{5,6},{6,7},{7,8},{8,9},{9,10},{10,1... | collective-permute-start | bytes 98312 | tf_op jit(solution)/shard_map/ppermute | solution.py:84
  23.0 6.5 %collective-permute-start.1 = (bf16[8,2048]{1,0:T(8,128)(2,1)S(1)}, bf16[8,2048]{1,0:T(8,128)(2,1)S(1)}, u32[]{:S(2)}, u32[]{:S(2)}) collective-permute-start(bf16[8,2048]{1,0:T(8,128)(2,1)S(1)} %collective-permute-done), channel_id=1, source_target_pairs={{0,1},{1,2},{2,3},{3,4},{4,5},{5,6},{6,7},{7,8},{8,9},{9,10},{10,1... | collective-permute-start | bytes 98312 | tf_op jit(solution)/shard_map/ppermute | solution.py:84
  29.6 6.6 %collective-permute-start.2 = (bf16[8,2048]{1,0:T(8,128)(2,1)S(1)}, bf16[8,2048]{1,0:T(8,128)(2,1)S(1)}, u32[]{:S(2)}, u32[]{:S(2)}) collective-permute-start(bf16[8,2048]{1,0:T(8,128)(2,1)S(1)} %collective-permute-done.1), channel_id=1, source_target_pairs={{0,1},{1,2},{2,3},{3,4},{4,5},{5,6},{6,7},{7,8},{8,9},{9,10},{10,1... | collective-permute-start | bytes 98312 | tf_op jit(solution)/shard_map/ppermute | solution.py:84
  36.1 6.0 %collective-permute-start.3 = (bf16[8,2048]{1,0:T(8,128)(2,1)S(1)}, bf16[8,2048]{1,0:T(8,128)(2,1)S(1)}, u32[]{:S(2)}, u32[]{:S(2)}) collective-permute-start(bf16[8,2048]{1,0:T(8,128)(2,1)S(1)} %collective-permute-done.2), channel_id=1, source_target_pairs={{0,1},{1,2},{2,3},{3,4},{4,5},{5,6},{6,7},{7,8},{8,9},{9,10},{10,1... | collective-permute-start | bytes 98312 | tf_op jit(solution)/shard_map/ppermute | solution.py:84
  42.2 6.8 %collective-permute-start.4 = (bf16[8,2048]{1,0:T(8,128)(2,1)S(1)}, bf16[8,2048]{1,0:T(8,128)(2,1)S(1)}, u32[]{:S(2)}, u32[]{:S(2)}) collective-permute-start(bf16[8,2048]{1,0:T(8,128)(2,1)S(1)} %collective-permute-done.3), channel_id=1, source_target_pairs={{0,1},{1,2},{2,3},{3,4},{4,5},{5,6},{6,7},{7,8},{8,9},{9,10},{10,1... | collective-permute-start | bytes 98312 | tf_op jit(solution)/shard_map/ppermute | solution.py:84
  48.9 6.7 %collective-permute-start.5 = (bf16[8,2048]{1,0:T(8,128)(2,1)S(1)}, bf16[8,2048]{1,0:T(8,128)(2,1)S(1)}, u32[]{:S(2)}, u32[]{:S(2)}) collective-permute-start(bf16[8,2048]{1,0:T(8,128)(2,1)S(1)} %collective-permute-done.4), channel_id=1, source_target_pairs={{0,1},{1,2},{2,3},{3,4},{4,5},{5,6},{6,7},{7,8},{8,9},{9,10},{10,1... | collective-permute-start | bytes 98312 | tf_op jit(solution)/shard_map/ppermute | solution.py:84
  56.2 6.6 %collective-permute-start.6 = (bf16[8,2048]{1,0:T(8,128)(2,1)S(1)}, bf16[8,2048]{1,0:T(8,128)(2,1)S(1)}, u32[]{:S(2)}, u32[]{:S(2)}) collective-permute-start(bf16[8,2048]{1,0:T(8,128)(2,1)S(1)} %collective-permute-done.5), channel_id=1, source_target_pairs={{0,1},{1,2},{2,3},{3,4},{4,5},{5,6},{6,7},{7,8},{8,9},{9,10},{10,1... | collective-permute-start | bytes 98312 | tf_op jit(solution)/shard_map/ppermute | solution.py:84
  63.4 6.0 %collective-permute-start.7 = (bf16[8,2048]{1,0:T(8,128)(2,1)S(1)}, bf16[8,2048]{1,0:T(8,128)(2,1)S(1)}, u32[]{:S(2)}, u32[]{:S(2)}) collective-permute-start(bf16[8,2048]{1,0:T(8,128)(2,1)S(1)} %collective-permute-done.6), channel_id=1, source_target_pairs={{0,1},{1,2},{2,3},{3,4},{4,5},{5,6},{6,7},{7,8},{8,9},{9,10},{10,1... | collective-permute-start | bytes 98312 | tf_op jit(solution)/shard_map/ppermute | solution.py:84
  70.1 6.7 %collective-permute-start.8 = (bf16[8,2048]{1,0:T(8,128)(2,1)S(1)}, bf16[8,2048]{1,0:T(8,128)(2,1)S(1)}, u32[]{:S(2)}, u32[]{:S(2)}) collective-permute-start(bf16[8,2048]{1,0:T(8,128)(2,1)S(1)} %collective-permute-done.7), channel_id=1, source_target_pairs={{0,1},{1,2},{2,3},{3,4},{4,5},{5,6},{6,7},{7,8},{8,9},{9,10},{10,1... | collective-permute-start | bytes 98312 | tf_op jit(solution)/shard_map/ppermute | solution.py:84
  76.8 27.0 %copy-start.11 = (bf16[8,2048]{1,0:T(8,128)(2,1)}, bf16[8,2048]{1,0:T(8,128)(2,1)S(1)}, u32[]{:S(2)}) copy-start(bf16[8,2048]{1,0:T(8,128)(2,1)S(1)} %collective-permute-done.8) | copy-start | bytes 98308
  76.8 6.7 %collective-permute-start.9 = (bf16[8,2048]{1,0:T(8,128)(2,1)S(1)}, bf16[8,2048]{1,0:T(8,128)(2,1)S(1)}, u32[]{:S(2)}, u32[]{:S(2)}) collective-permute-start(bf16[8,2048]{1,0:T(8,128)(2,1)S(1)} %collective-permute-done.8), channel_id=1, source_target_pairs={{0,1},{1,2},{2,3},{3,4},{4,5},{5,6},{6,7},{7,8},{8,9},{9,10},{10,1... | collective-permute-start | bytes 98312 | tf_op jit(solution)/shard_map/ppermute | solution.py:84
  83.5 20.3 %copy-start.12 = (bf16[8,2048]{1,0:T(8,128)(2,1)}, bf16[8,2048]{1,0:T(8,128)(2,1)S(1)}, u32[]{:S(2)}) copy-start(bf16[8,2048]{1,0:T(8,128)(2,1)S(1)} %collective-permute-done.9) | copy-start | bytes 98308
  83.5 6.7 %collective-permute-start.10 = (bf16[8,2048]{1,0:T(8,128)(2,1)S(1)}, bf16[8,2048]{1,0:T(8,128)(2,1)S(1)}, u32[]{:S(2)}, u32[]{:S(2)}) collective-permute-start(bf16[8,2048]{1,0:T(8,128)(2,1)S(1)} %collective-permute-done.9), channel_id=1, source_target_pairs={{0,1},{1,2},{2,3},{3,4},{4,5},{5,6},{6,7},{7,8},{8,9},{9,10},{10,1... | collective-permute-start | bytes 98312 | tf_op jit(solution)/shard_map/ppermute | solution.py:84
  90.2 6.7 %collective-permute-start.11 = (bf16[8,2048]{1,0:T(8,128)(2,1)S(1)}, bf16[8,2048]{1,0:T(8,128)(2,1)S(1)}, u32[]{:S(2)}, u32[]{:S(2)}) collective-permute-start(bf16[8,2048]{1,0:T(8,128)(2,1)S(1)} %collective-permute-done.10), channel_id=1, source_target_pairs={{0,1},{1,2},{2,3},{3,4},{4,5},{5,6},{6,7},{7,8},{8,9},{9,10},{10,1... | collective-permute-start | bytes 98312 | tf_op jit(solution)/shard_map/ppermute | solution.py:84
  96.9 6.9 %collective-permute-start.12 = (bf16[8,2048]{1,0:T(8,128)(2,1)S(1)}, bf16[8,2048]{1,0:T(8,128)(2,1)}, u32[]{:S(2)}, u32[]{:S(2)}) collective-permute-start(bf16[8,2048]{1,0:T(8,128)(2,1)S(1)} %collective-permute-done.11), channel_id=1, source_target_pairs={{0,1},{1,2},{2,3},{3,4},{4,5},{5,6},{6,7},{7,8},{8,9},{9,10},{10,1... | collective-permute-start | bytes 98312 | tf_op jit(solution)/shard_map/ppermute | solution.py:84
  103.8 7.0 %collective-permute-start.13 = (bf16[8,2048]{1,0:T(8,128)(2,1)}, bf16[8,2048]{1,0:T(8,128)(2,1)}, u32[]{:S(2)}, u32[]{:S(2)}) collective-permute-start(bf16[8,2048]{1,0:T(8,128)(2,1)} %collective-permute-done.12), channel_id=1, source_target_pairs={{0,1},{1,2},{2,3},{3,4},{4,5},{5,6},{6,7},{7,8},{8,9},{9,10},{10,1... | collective-permute-start | bytes 98312 | tf_op jit(solution)/shard_map/ppermute | solution.py:84
  110.8 6.4 %collective-permute-start.14 = (bf16[8,2048]{1,0:T(8,128)(2,1)}, bf16[8,2048]{1,0:T(8,128)(2,1)}, u32[]{:S(2)}, u32[]{:S(2)}) collective-permute-start(bf16[8,2048]{1,0:T(8,128)(2,1)} %collective-permute-done.13), channel_id=1, source_target_pairs={{0,1},{1,2},{2,3},{3,4},{4,5},{5,6},{6,7},{7,8},{8,9},{9,10},{10,1... | collective-permute-start | bytes 98312 | tf_op jit(solution)/shard_map/ppermute | solution.py:84
  141.7 69.1 %copy-start.16 = (pred[256]{0:T(512)(128)(4,1)S(1)}, pred[256]{0:T(512)(128)(4,1)}, u32[]{:S(2)}) copy-start(pred[256]{0:T(512)(128)(4,1)} %copy-done.15) | copy-start | bytes 772
  (13 other events, 51.6 us)
Sparse Core Ops, SparseCore 0:
  10.2 101.5 all-gather.2
  114.7 96.0 all-gather.4
